TPU v7x, 32 devices: a whole 2x2x4 slice. The times are simulated.
32 devices in a mesh: space: 8 (over z, x), fsdp: 4 (over y, core).
Axes of the slice: x: 2, y: 2, z: 4, core: 2. Of those that a mesh axis runs over, the one named last changes fastest.
Arguments:
- features: bfloat16 [4, 128, 8, 8, 512], P('fsdp', 'space'), may hold values from -6 to 6
- cotangent: bfloat16 [4, 128, 8, 8, 512], P('fsdp', 'space'), may hold values from -6 to 6
- tissue: int32 [4, 128], P('fsdp', 'space'), may hold values 0 or 1
- weight: bfloat16 [27, 64, 64], P(None, 'fsdp'), may hold values from -0.15625 to 0.15625
Outputs:
- activations: bfloat16 [4, 128, 8, 8, 512], P('fsdp', 'space')
- input_grad: bfloat16 [4, 128, 8, 8, 512], P('fsdp', 'space')
- weight_grad: float32 [27, 64, 64], P(None, 'fsdp')
All inputs are finite; a program needn't handle non-finite values. No bound on the sum of `tissue` on one device may be relied on, other than what follows from the above.
Results may differ from a plain program's by a relative error of at most 0.0034.
Values may be sent and summed in bfloat16 or wider, within the bound.
No kernel may reach another device: no remote copies, remote signals or barrier semaphores. Data moves between devices by JAX's collectives and lax.ppermute only.
A program may use at most 192 MiB of HBM per device.

v0:
```python
import math
import jax
import jax.numpy as jnp
from jax import lax
from jax.sharding import PartitionSpec as P

BRICK_X = 2
BRICK_Y = 2
BRICK_Z = 4
PAIR = 2
DEPTH = 2
CONV_DIMS = ("NDHWC", "DHWIO", "NDHWC")


def from_behind(shard, axis, by):
    peers = lax.axis_size(axis)
    pairs = [(i, i + by) for i in range(peers) if 0 <= i + by < peers]
    return lax.ppermute(shard, axis, pairs)


def grid_shape(number):
    factors = [1, 1, 1]
    places = 0
    while number % 2 == 0:
        factors[places % 3] = factors[places % 3] * 2
        number = number // 2
        places = places + 1
    factors[0] = factors[0] * number
    return factors


def to_volume(bricks, edge_cells, lanes):
    per_brick = edge_cells // PAIR
    blocks = bricks.reshape(BRICK_X, BRICK_Y, BRICK_Z, edge_cells, edge_cells, per_brick, lanes)
    blocks = blocks.transpose(0, 3, 1, 4, 2, 5, 6)
    return blocks.reshape(BRICK_X * edge_cells, BRICK_Y * edge_cells, BRICK_Z * per_brick, lanes)


def to_bricks(volume, edge_cells, lanes):
    per_brick = edge_cells // PAIR
    blocks = volume.reshape(BRICK_X, edge_cells, BRICK_Y, edge_cells, BRICK_Z, per_brick, lanes)
    blocks = blocks.transpose(0, 2, 4, 1, 3, 5, 6)
    return blocks.reshape(BRICK_X * BRICK_Y * BRICK_Z, edge_cells, edge_cells, per_brick * lanes)


def neighbour_plane(portion, offset, present):
    arrived = from_behind(portion, "space", offset)
    return jnp.where(present, arrived, jnp.zeros_like(arrived))


def extend(volume, grid_dims, places, widths):
    strides = (grid_dims[1] * grid_dims[2], grid_dims[2], 1)
    for axis_pos in range(3):
        axis = axis_pos + 1
        extent = volume.shape[axis]
        width = widths[axis_pos]
        last_layer = lax.slice_in_dim(volume, extent - width, extent, axis=axis)
        first_layer = lax.slice_in_dim(volume, 0, width, axis=axis)
        from_below = neighbour_plane(last_layer, strides[axis_pos], places[axis_pos] > 0)
        from_above = neighbour_plane(
            first_layer, -strides[axis_pos], places[axis_pos] < grid_dims[axis_pos] - 1
        )
        volume = jnp.concatenate([from_below, volume, from_above], axis=axis)
    return volume


def super_kernel(weight_full, channels):
    taps = weight_full.reshape(3, 3, 3, channels, channels)
    zero = jnp.zeros((3, 3, channels, channels), weight_full.dtype)
    rows = []
    for dz in range(3):
        row = []
        for hi in range(PAIR):
            col = []
            for ho in range(PAIR):
                c = 2 * dz - 1 + hi - ho
                col.append(taps[:, :, c] if 0 <= c < 3 else zero)
            row.append(jnp.concatenate(col, axis=-1))
        rows.append(jnp.concatenate(row, axis=-2))
    return jnp.stack(rows, axis=2)


def fold_kernel_grad(grad_sup, channels):
    taps = [None, None, None]
    for dz in range(3):
        for hi in range(PAIR):
            for ho in range(PAIR):
                c = 2 * dz - 1 + hi - ho
                if 0 <= c < 3:
                    block = grad_sup[
                        :,
                        :,
                        dz,
                        hi * channels : (hi + 1) * channels,
                        ho * channels : (ho + 1) * channels,
                    ]
                    taps[c] = block if taps[c] is None else taps[c] + block
    return jnp.stack(taps, axis=2).reshape(27, channels, channels)


def conv(volume, kernel):
    return lax.conv_general_dilated(
        volume[None],
        kernel,
        (1, 1, 1),
        "VALID",
        dimension_numbers=CONV_DIMS,
        preferred_element_type=jnp.float32,
    )[0]


def kernel_grad(inputs, grads):
    out = lax.conv_general_dilated(
        inputs[None],
        grads[None],
        (1, 1, 1),
        "VALID",
        dimension_numbers=("CDHWN", "IDHWO", "NDHWC"),
        preferred_element_type=jnp.float32,
    )
    return out.transpose(1, 2, 3, 0, 4)


def local(features, cotangent, tissue, weight):
    edge_cells = features.shape[2]
    channels = weight.shape[2]
    lanes = PAIR * channels
    grid_dims = grid_shape(lax.axis_size("space"))
    index_now = lax.axis_index("space")
    places = (
        index_now // (grid_dims[1] * grid_dims[2]),
        index_now // grid_dims[2] % grid_dims[1],
        index_now % grid_dims[2],
    )
    weight_full = lax.all_gather(weight, "fsdp", axis=1, tiled=True)
    k_fwd = super_kernel(weight_full, channels)
    k_back = jnp.flip(k_fwd, (0, 1, 2)).transpose(0, 1, 2, 4, 3)
    present = tissue[0][:, None, None, None] > 0
    inputs = features[0]
    incoming = cotangent[0]
    masked = jnp.where(present, inputs, jnp.zeros_like(inputs))
    masked_cot = jnp.where(present, incoming, jnp.zeros_like(incoming))
    both = jnp.stack(
        [to_volume(masked, edge_cells, lanes), to_volume(masked_cot, edge_cells, lanes)]
    )
    grown = extend(both, grid_dims, places, (DEPTH, DEPTH, 1))
    grown = jnp.pad(grown, ((0, 0), (0, 0), (0, 0), (1, 1), (0, 0)))
    padded_in = grown[0]
    cot_ext = grown[1, 1:-1, 1:-1, 1:-1]
    pre_ext = conv(padded_in, k_fwd)
    gate_ext = jax.nn.sigmoid(pre_ext)
    slope_ext = gate_ext * (1.0 + pre_ext * (1.0 - gate_ext))
    grad_ext = (cot_ext.astype(jnp.float32) * slope_ext).astype(jnp.bfloat16)
    tissue_mask = tissue[0].astype(jnp.float32)[:, None, None, None]
    pre = to_bricks(pre_ext[1:-1, 1:-1, 1:-1], edge_cells, lanes)
    gate_val = to_bricks(gate_ext[1:-1, 1:-1, 1:-1], edge_cells, lanes)
    activations = (tissue_mask * (inputs.astype(jnp.float32) + pre * gate_val)).astype(jnp.bfloat16)
    back = to_bricks(conv(grad_ext, k_back), edge_cells, lanes)
    input_grad = (tissue_mask * (incoming.astype(jnp.float32) + back)).astype(jnp.bfloat16)
    total_cells = (
        lax.axis_size("space") * lax.axis_size("fsdp") * BRICK_X * BRICK_Y * BRICK_Z * edge_cells**3
    )
    grad_sup = kernel_grad(padded_in[1:-1, 1:-1, 1:-1], grad_ext[1:-1, 1:-1, 1:-1])
    grad_term = fold_kernel_grad(grad_sup, channels) / math.sqrt(total_cells)
    grad_part = lax.psum_scatter(grad_term, "fsdp", scatter_dimension=1, tiled=True)
    grad_part = lax.psum(grad_part, "space")
    return (activations[None], input_grad[None], grad_part)


def solution(mesh):
    return jax.shard_map(
        local,
        mesh=mesh,
        in_specs=(
            P("fsdp", "space", None, None, None),
            P("fsdp", "space", None, None, None),
            P("fsdp", "space"),
            P(None, "fsdp", None),
        ),
        out_specs=(
            P("fsdp", "space", None, None, None),
            P("fsdp", "space", None, None, None),
            P(None, "fsdp", None),
        ),
        check_vma=False,
    )
```

profile of v0, /device:TPU:0, one launch (start us, length us, event | category | flops | bytes accessed | tf_op | source)
XLA Modules:
  0.0 291.2 jit_solution(907447351510930595)
XLA Ops:
  7.2 0.0 reduce-scatter.2.cloned.1.call-start
  7.2 0.7 compare_reduce_fusion
  7.9 0.1 gt.24
  8.0 2.7 copy_select_fusion.1
  10.7 1.3 collective-permute-start.1
  12.0 6.7 %collective-permute-start = (bf16[2,2,16,16,128]{4,3,2,1,0:T(8,128)(2,1)S(1)}, bf16[2,2,16,16,128]{4,3,2,1,0:T(8,128)(2,1)S(1)}, u32[]{:S(2)}, u32[]{:S(2)}) collective-permute-start(bf16[2,2,16,16,128]{4,3,2,1,0:T(8,128)(2,1)S(1)} %get-tuple-element.11), channel_id=1, source_target_pairs={{0,16},{4,20},{8,24},{12,28},{1,17},{5,21},{9,25},{13,29},{2,18},{... | collective-permute-start | bytes 786440 | tf_op jit(solution)/shard_map/ppermute | solution.py:18
  18.7 7.7 %all_gather.3 = bf16[27,64,64]{2,1,0:T(8,128)(2,1)S(1)} all-gather(bf16[27,16,64]{2,1,0:T(8,128)(2,1)S(1)} %copy-done.14), channel_id=1, replica_groups=mesh['space'=8,'fsdp'=4] {'fsdp'}, dimensions={1}, use_global_device_ids=true | all-gather | bytes 276480 | tf_op jit(solution)/shard_map/all_gather | solution.py:135
  26.4 1.7 collective-permute-done.1
  28.1 1.0 broadcast_select_fusion.5
  29.1 0.1 pad_maximum_fusion.13
  29.2 1.3 collective-permute-start.3
  30.6 4.8 %collective-permute-start.2 = (bf16[2,20,2,16,128]{4,3,2,1,0:T(8,128)(2,1)S(1)}, bf16[2,20,2,16,128]{4,3,2,1,0:T(8,128)(2,1)S(1)}, u32[]{:S(2)}, u32[]{:S(2)}) collective-permute-start(bf16[2,20,2,16,128]{4,3,2,1,0:T(8,128)(2,1)S(1)} %get-tuple-element.9), channel_id=1, source_target_pairs={{0,8},{4,12},{8,16},{12,20},{16,24},{20,28},{1,9},{5,13},{9,17},{1... | collective-permute-start | bytes 983048 | tf_op jit(solution)/shard_map/ppermute | solution.py:18
  35.3 0.3 pad_bitcast_fusion.1
  35.7 5.6 %collective-permute-done.3 = bf16[2,20,2,16,128]{4,3,2,1,0:T(8,128)(2,1)S(1)} collective-permute-done((bf16[2,20,2,16,128]{4,3,2,1,0:T(8,128)(2,1)S(1)}, bf16[2,20,2,16,128]{4,3,2,1,0:T(8,128)(2,1)S(1)}, u32[]{:S(2)}, u32[]{:S(2)}) %collective-permute-start.3) | collective-permute-done | bytes 327712 | tf_op jit(solution)/shard_map/ppermute | solution.py:18
  41.3 1.2 collective-permute-done.2
  42.5 1.9 pad_maximum_fusion.7
  44.4 1.3 collective-permute-start.5
  45.7 0.5 convert_bitcast_fusion.1
  46.2 4.7 %collective-permute-start.4 = (bf16[2,20,20,1,128]{4,3,2,1,0:T(2,128)(2,1)S(1)}, bf16[2,20,20,1,128]{4,3,2,1,0:T(2,128)(2,1)S(1)}, u32[]{:S(2)}, u32[]{:S(2)}) collective-permute-start(bf16[2,20,20,1,128]{4,3,2,1,0:T(2,128)(2,1)S(1)} %get-tuple-element.7), channel_id=1, source_target_pairs={{0,4},{4,8},{8,12},{12,16},{16,20},{20,24},{24,28},{1,5},{5,9},{9,... | collective-permute-start | bytes 614408 | tf_op jit(solution)/shard_map/ppermute | solution.py:18
  50.9 6.3 %collective-permute-done.5 = bf16[2,20,20,1,128]{4,3,2,1,0:T(2,128)(2,1)S(1)} collective-permute-done((bf16[2,20,20,1,128]{4,3,2,1,0:T(2,128)(2,1)S(1)}, bf16[2,20,20,1,128]{4,3,2,1,0:T(2,128)(2,1)S(1)}, u32[]{:S(2)}, u32[]{:S(2)}) %collective-permute-start.5) | collective-permute-done | bytes 204832 | tf_op jit(solution)/shard_map/ppermute | solution.py:18
  57.2 0.4 broadcast_select_fusion.1
  57.7 8.5 %collective-permute-done.4 = bf16[2,20,20,1,128]{4,3,2,1,0:T(2,128)(2,1)S(1)} collective-permute-done((bf16[2,20,20,1,128]{4,3,2,1,0:T(2,128)(2,1)S(1)}, bf16[2,20,20,1,128]{4,3,2,1,0:T(2,128)(2,1)S(1)}, u32[]{:S(2)}, u32[]{:S(2)}) %collective-permute-start.4) | collective-permute-done | bytes 204832 | tf_op jit(solution)/shard_map/ppermute | solution.py:18
  66.2 0.4 broadcast_select_fusion.2
  66.6 5.9 %pad_maximum_fusion = bf16[2,20,20,18,128]{4,3,2,1,0:T(8,128)(2,1)S(1)} fusion(bf16[2,20,20,1,128]{4,3,2,1,0:T(2,128)(2,1)S(1)} %broadcast_select_fusion.1, bf16[2,20,2,16,128]{4,3,2,1,0:T(8,128)(2,1)S(1)} %broadcast_select_fusion.3, bf16[2,2,16,16,128]{4,3,2,1,0:T(8,128)(2,1)S(1)} %broadcast_select_fusion.5, bf16[1,16,16,16,128]{4,3,2,1,0:T(8,128)(2,1)S(1)} %bitcast.89, ...), kind=kLoop, calls=%fused_computation.6 | loop fusion | flops 29491200 | bytes 7372800 | tf_op jit(solution)/shard_map/concatenate | solution.py:63
  72.5 3.0 %fusion.29 = (bf16[20,20,20,128]{3,2,1,0:T(8,128)(2,1)}, bf16[20,20,1,20,128]{4,3,1,0,2:T(8,128)(2,1)S(1)}) fusion(bf16[2,20,20,18,128]{4,3,2,1,0:T(8,128)(2,1)S(1)} %pad_maximum_fusion), kind=kLoop, calls=%fused_computation.39 | loop fusion | bytes 7782400 | tf_op jit(solution)/shard_map/squeeze | solution.py:148
  75.5 0.4 copy.52
  75.8 0.7 pad.9.clone
  76.6 0.3 copy.34
  76.9 0.5 slice.93
  77.5 17.0 %add_multiply_fusion = (f32[18,18,8,3,128]{4,2,3,1,0:T(8,128)}, f32[18,18,8,3,128]{4,2,3,1,0:T(8,128)S(1)}) fusion(bf16[3,3,1,128,128]{4,3,2,1,0:T(8,128)(2,1)S(1)} %get-tuple-element.21, bf16[3,3,1,128,128]{4,3,2,1,0:T(8,128)(2,1)S(1)} %get-tuple-element.20, bf16[3,3,1,128,128]{4,3,2,1,0:T(8,128)(2,1)S(1)} %get-tuple-element.19, ...), kind=kOutput, calls=%fused_computation.17 | convolution fusion | flops 6900842496 | bytes 12738584 | tf_op jit(solution)/shard_map/conv_general_dilated | solution.py:102
  94.4 4.0 %copy.40 = f32[18,18,8,3,128]{4,3,2,1,0:T(4,128)} copy(f32[18,18,8,3,128]{4,2,3,1,0:T(8,128)S(1)} %get-tuple-element.27) | data formatting | bytes 7962624 | tf_op jit(solution)/shard_map/conv_general_dilated | solution.py:102
  98.4 7.3 %reshape.72 = f32[18,18,1,24,128]{4,3,1,0,2:T(8,128)} reshape(f32[18,18,8,3,128]{4,3,2,1,0:T(4,128)} %copy.40) | data formatting | bytes 7962624 | tf_op jit(solution)/shard_map/conv_general_dilated | solution.py:102
  105.7 4.5 %slice_bitcast_fusion.1 = f32[18,18,18,128]{3,2,1,0:T(8,128)} fusion(f32[18,18,1,24,128]{4,3,1,0,2:T(8,128)} %reshape.72), kind=kLoop, calls=%fused_computation.16 | loop fusion | bytes 5971968 | tf_op jit(solution)/shard_map/squeeze | solution.py:102
  110.2 3.0 %add_divide_fusion = f32[18,18,18,128]{3,2,1,0:T(8,128)} fusion(f32[18,18,1,24,128]{4,3,1,0,2:T(8,128)S(1)} %copy-done.1), kind=kLoop, calls=%fused_computation.18 | loop fusion | flops 2239488 | bytes 5971968 | tf_op jit(solution)/shard_map/div | solution.py:151
  113.2 3.9 %convert_bitcast_fusion = f32[18,18,18,128]{3,2,1,0:T(8,128)} fusion(bf16[2,20,20,18,128]{4,3,2,1,0:T(8,128)(2,1)} %copy-done), kind=kLoop, calls=%fused_computation.4 | loop fusion | flops 746496 | bytes 4478976 | tf_op jit(solution)/shard_map/convert_element_type | solution.py:153
  117.1 4.0 %copy.42 = f32[18,18,8,3,128]{4,3,2,1,0:T(4,128)} copy(f32[18,18,8,3,128]{4,2,3,1,0:T(8,128)S(1)} %copy-done.9) | data formatting | bytes 7962624 | tf_op jit(solution)/shard_map/mul | solution.py:152
  121.0 7.3 %reshape.81 = f32[18,18,1,24,128]{4,3,1,0,2:T(8,128)} reshape(f32[18,18,8,3,128]{4,3,2,1,0:T(4,128)} %copy.42) | data formatting | bytes 7962624 | tf_op jit(solution)/shard_map/mul | solution.py:152
  128.3 3.2 %fusion.22 = bf16[18,18,1,18,128]{4,3,1,0,2:T(8,128)(2,1)S(1)} fusion(f32[18,18,1,24,128]{4,3,1,0,2:T(8,128)} %reshape.81, bf16[2,20,20,18,128]{4,3,2,1,0:T(8,128)(2,1)} %copy-done), kind=kLoop, calls=%fused_computation.33 | loop fusion | flops 2239488 | bytes 5971968 | tf_op jit(solution)/shard_map/convert_element_type | solution.py:153
  131.5 1.6 pad.11
  133.1 5.5 %reshape.75 = bf16[18,18,1,8,3,128]{5,4,3,1,0,2:T(4,128)(2,1)S(1)} reshape(bf16[18,18,1,24,128]{4,3,1,0,2:T(8,128)(2,1)} %pad.11) | data formatting | bytes 3981312 | tf_op jit(solution)/shard_map/conv_general_dilated | solution.py:102
  138.7 0.3 copy.44
  139.1 1.3 copy-done.6
  140.3 1.5 slice.102
  141.9 1.1 slice_bitcast_fusion.2
  143.0 1.2 copy-done.2
  144.1 4.3 %fusion.31 = (bf16[1,16,16,16,128]{4,3,2,1,0:T(8,128)(2,1)S(1)}, f32[16,16,16,128]{3,2,1,0:T(8,128)}) fusion(f32[18,18,18,128]{3,2,1,0:T(8,128)S(1)} %copy-done.2, f32[18,18,18,128]{3,2,1,0:T(8,128)S(1)} %copy-done.3, f32[18,18,18,128]{3,2,1,0:T(8,128)} %convert_bitcast_fusion), kind=kLoop, calls=%fused_computation.41 | loop fusion | flops 3670016 | bytes 9437184 | tf_op jit(solution)/shard_map/broadcast_in_dim | solution.py:115
  148.4 32.2 %fusion.17 = f32[3,3,3,128,128]{4,3,2,1,0:T(8,128)S(1)} fusion(bf16[1,18,18,18,128]{4,3,2,1,0:T(8,128)(2,1)S(1)} %slice_bitcast_fusion.2, bf16[1,16,16,16,128]{4,3,2,1,0:T(8,128)(2,1)S(1)} %get-tuple-element.3), kind=kOutput, calls=%fused_computation.25 | convolution fusion | flops 3623878656 | bytes 4311040 | tf_op jit(solution)/shard_map/transpose | solution.py:121
  180.7 0.3 slice_add_fusion.2
  181.0 1.0 maximum_multiply_fusion
  182.0 0.0 reduce-scatter.2.cloned.1.call-update
  182.0 0.3 all-reduce.7.cloned.1.call-start
  182.3 0.2 copy-done.7
  182.6 0.4 copy-done.10
  182.9 13.3 %fusion.25 = f32[16,16,8,3,128]{4,2,3,1,0:T(8,128)S(1)} fusion(bf16[18,18,1,7,2,128]{5,3,4,1,0,2:T(8,128)(2,1)S(1)} %copy-done.10, bf16[18,18,1,8,3,128]{5,3,4,1,0,2:T(8,128)(2,1)S(1)} %copy-done.7, pred[8,3]{0,1:T(4,128)(4,1)S(1)} %copy-done.17, bf16[3,3,1,128,128]{4,3,2,1,0:T(8,128)(2,1)} %copy-done.13, bf16[3,3,1,128,128]{4,3,2,1,0:T(8,128)(2,1)} %copy-done.12, ...), kind=kOutput, calls=%fused_computation.37 | convolution fusion | flops 5447442432 | bytes 7182360 | tf_op jit(solution)/shard_map/conv_general_dilated | solution.py:102
  196.3 0.5 copy.45
  196.8 0.1 slice.103
  197.0 0.3 copy.46
  197.3 1.1 copy-done.4
  198.4 2.0 copy.41
  200.4 7.6 %reduce-scatter.2.cloned.1.call-done = f32[27,16,64]{2,1,0:T(8,128)} async-done(((f32[27,64,64]{2,1,0:T(8,128)}), f32[27,16,64]{2,1,0:T(8,128)}) %reduce-scatter.2.cloned.1.call-update) | async-done | bytes 110608 | tf_op jit(solution)/shard_map/reduce_scatter | solution.py:165
  208.0 0.0 all-reduce.7.cloned.1.call-update
  208.1 4.2 %multiply_convert_fusion = (bf16[1,16,8,8,512]{4,3,2,1,0:T(8,128)(2,1)}, bf16[1,16,8,8,512]{4,3,2,1,0:T(8,128)(2,1)}) fusion(f32[1,16,8,8,512]{4,3,2,1,0:T(8,128)S(1)} %bitcast.94, bf16[1,16,8,8,512]{4,3,2,1,0:T(8,128)(2,1)} %param.5, f32[16]{0:T(128)S(1)} %copy-done.15, f32[1,16,8,8,512]{4,3,2,1,0:T(8,128)} %bitcast.95, ...), kind=kLoop, calls=%fused_computation.29 | loop fusion | flops 4194304 | bytes 8388672 | tf_op jit(solution)/shard_map/convert_element_type | solution.py:159
  212.3 70.0 %all-reduce.7.cloned.1.call-done = f32[27,16,64]{2,1,0:T(8,128)} async-done(((f32[27,16,64]{2,1,0:T(8,128)}), f32[27,16,64]{2,1,0:T(8,128)}) %all-reduce.7.cloned.1.call-update) | async-done | bytes 110608 | tf_op jit(solution)/shard_map/psum | solution.py:166
  282.2 1.6 copy.60
  (39 shorter events, 0.2 us)
Async XLA Ops:
  7.2 11.5 %copy-start.14 = (bf16[27,16,64]{2,1,0:T(8,128)(2,1)S(1)}, bf16[27,16,64]{2,1,0:T(8,128)(2,1)}, u32[]{:S(2)}) copy-start(bf16[27,16,64]{2,1,0:T(8,128)(2,1)} %param.7) | copy-start | bytes 165892
  7.2 200.8 %reduce-scatter.2.cloned.1.call-start = ((), (), s32[]{:S(2)}) async-start(), calls=%async_computation.1 | async-start | bytes 1105920 | tf_op jit(solution)/shard_map/reduce_scatter | solution.py:165
  10.7 17.4 %collective-permute-start.1 = (bf16[2,2,16,16,128]{4,3,2,1,0:T(8,128)(2,1)S(1)}, bf16[2,2,16,16,128]{4,3,2,1,0:T(8,128)(2,1)}, u32[]{:S(2)}, u32[]{:S(2)}) collective-permute-start(bf16[2,2,16,16,128]{4,3,2,1,0:T(8,128)(2,1)S(1)} %get-tuple-element.12), channel_id=1, source_target_pairs={{16,0},{20,4},{24,8},{28,12},{17,1},{21,5},{25,9},{29,13},{18,2},{... | collective-permute-start | bytes 786440 | tf_op jit(solution)/shard_map/ppermute | solution.py:18
  12.0 17.0 %collective-permute-start = (bf16[2,2,16,16,128]{4,3,2,1,0:T(8,128)(2,1)S(1)}, bf16[2,2,16,16,128]{4,3,2,1,0:T(8,128)(2,1)S(1)}, u32[]{:S(2)}, u32[]{:S(2)}) collective-permute-start(bf16[2,2,16,16,128]{4,3,2,1,0:T(8,128)(2,1)S(1)} %get-tuple-element.11), channel_id=1, source_target_pairs={{0,16},{4,20},{8,24},{12,28},{1,17},{5,21},{9,25},{13,29},{2,18},{... | collective-permute-start | bytes 786440 | tf_op jit(solution)/shard_map/ppermute | solution.py:18
  29.2 16.5 %copy-start.16 = (s32[1,16]{1,0:T(1,128)S(1)}, s32[1,16]{1,0:T(1,128)}, u32[]{:S(2)}) copy-start(s32[1,16]{1,0:T(1,128)} %param.6) | copy-start | bytes 196
  29.2 12.0 %collective-permute-start.3 = (bf16[2,20,2,16,128]{4,3,2,1,0:T(8,128)(2,1)S(1)}, bf16[2,20,2,16,128]{4,3,2,1,0:T(8,128)(2,1)S(1)}, u32[]{:S(2)}, u32[]{:S(2)}) collective-permute-start(bf16[2,20,2,16,128]{4,3,2,1,0:T(8,128)(2,1)S(1)} %get-tuple-element.10), channel_id=1, source_target_pairs={{8,0},{12,4},{16,8},{20,12},{24,16},{28,20},{9,1},{13,5},{17,9},{2... | collective-permute-start | bytes 983048 | tf_op jit(solution)/shard_map/ppermute | solution.py:18
  30.6 11.9 %collective-permute-start.2 = (bf16[2,20,2,16,128]{4,3,2,1,0:T(8,128)(2,1)S(1)}, bf16[2,20,2,16,128]{4,3,2,1,0:T(8,128)(2,1)S(1)}, u32[]{:S(2)}, u32[]{:S(2)}) collective-permute-start(bf16[2,20,2,16,128]{4,3,2,1,0:T(8,128)(2,1)S(1)} %get-tuple-element.9), channel_id=1, source_target_pairs={{0,8},{4,12},{8,16},{12,20},{16,24},{20,28},{1,9},{5,13},{9,17},{1... | collective-permute-start | bytes 983048 | tf_op jit(solution)/shard_map/ppermute | solution.py:18
  35.6 41.8 %copy-start.11 = (bf16[3,3,1,128,128]{4,3,2,1,0:T(8,128)(2,1)}, bf16[3,3,1,128,128]{4,3,2,1,0:T(8,128)(2,1)S(1)}, u32[]{:S(2)}) copy-start(bf16[3,3,1,128,128]{4,3,2,1,0:T(8,128)(2,1)S(1)} %get-tuple-element.19) | copy-start | bytes 884740
  35.6 41.8 %copy-start.12 = (bf16[3,3,1,128,128]{4,3,2,1,0:T(8,128)(2,1)}, bf16[3,3,1,128,128]{4,3,2,1,0:T(8,128)(2,1)S(1)}, u32[]{:S(2)}) copy-start(bf16[3,3,1,128,128]{4,3,2,1,0:T(8,128)(2,1)S(1)} %get-tuple-element.20) | copy-start | bytes 884740
  35.6 41.8 %copy-start.13 = (bf16[3,3,1,128,128]{4,3,2,1,0:T(8,128)(2,1)}, bf16[3,3,1,128,128]{4,3,2,1,0:T(8,128)(2,1)S(1)}, u32[]{:S(2)}) copy-start(bf16[3,3,1,128,128]{4,3,2,1,0:T(8,128)(2,1)S(1)} %get-tuple-element.21) | copy-start | bytes 884740
  44.4 12.9 %collective-permute-start.5 = (bf16[2,20,20,1,128]{4,3,2,1,0:T(2,128)(2,1)S(1)}, bf16[2,20,20,1,128]{4,3,2,1,0:T(2,128)(2,1)S(1)}, u32[]{:S(2)}, u32[]{:S(2)}) collective-permute-start(bf16[2,20,20,1,128]{4,3,2,1,0:T(2,128)(2,1)S(1)} %get-tuple-element.8), channel_id=1, source_target_pairs={{4,0},{8,4},{12,8},{16,12},{20,16},{24,20},{28,24},{5,1},{9,5},{13... | collective-permute-start | bytes 614408 | tf_op jit(solution)/shard_map/ppermute | solution.py:18
  46.2 20.0 %collective-permute-start.4 = (bf16[2,20,20,1,128]{4,3,2,1,0:T(2,128)(2,1)S(1)}, bf16[2,20,20,1,128]{4,3,2,1,0:T(2,128)(2,1)S(1)}, u32[]{:S(2)}, u32[]{:S(2)}) collective-permute-start(bf16[2,20,20,1,128]{4,3,2,1,0:T(2,128)(2,1)S(1)} %get-tuple-element.7), channel_id=1, source_target_pairs={{0,4},{4,8},{8,12},{12,16},{16,20},{20,24},{24,28},{1,5},{5,9},{9,... | collective-permute-start | bytes 614408 | tf_op jit(solution)/shard_map/ppermute | solution.py:18
  72.5 3.0 %copy-start = (bf16[2,20,20,18,128]{4,3,2,1,0:T(8,128)(2,1)}, bf16[2,20,20,18,128]{4,3,2,1,0:T(8,128)(2,1)S(1)}, u32[]{:S(2)}) copy-start(bf16[2,20,20,18,128]{4,3,2,1,0:T(8,128)(2,1)S(1)} %pad_maximum_fusion) | copy-start | bytes 11059204
  76.6 0.8 copy-start.18
  105.7 4.5 %copy-start.1 = (f32[18,18,1,24,128]{4,3,1,0,2:T(8,128)S(1)}, f32[18,18,1,24,128]{4,3,1,0,2:T(8,128)}, u32[]{:S(2)}) copy-start(f32[18,18,1,24,128]{4,3,1,0,2:T(8,128)} %reshape.72) | copy-start | bytes 11943940
  113.2 3.9 %copy-start.9 = (f32[18,18,8,3,128]{4,2,3,1,0:T(8,128)S(1)}, f32[18,18,8,3,128]{4,2,3,1,0:T(8,128)}, u32[]{:S(2)}) copy-start(f32[18,18,8,3,128]{4,2,3,1,0:T(8,128)} %get-tuple-element.26) | copy-start | bytes 11943940
  138.7 3.2 %copy-start.5 = (bf16[20,20,20,128]{3,2,1,0:T(8,128)(2,1)S(1)}, bf16[20,20,20,128]{3,2,1,0:T(8,128)(2,1)}, u32[]{:S(2)}) copy-start(bf16[20,20,20,128]{3,2,1,0:T(8,128)(2,1)} %get-tuple-element.5) | copy-start | bytes 6144004
  138.7 4.3 %copy-start.3 = (f32[18,18,18,128]{3,2,1,0:T(8,128)S(1)}, f32[18,18,18,128]{3,2,1,0:T(8,128)}, u32[]{:S(2)}) copy-start(f32[18,18,18,128]{3,2,1,0:T(8,128)} %add_divide_fusion) | copy-start | bytes 8957956
  139.1 1.3 copy-start.6
  140.3 3.8 %copy-start.2 = (f32[18,18,18,128]{3,2,1,0:T(8,128)S(1)}, f32[18,18,18,128]{3,2,1,0:T(8,128)}, u32[]{:S(2)}) copy-start(f32[18,18,18,128]{3,2,1,0:T(8,128)} %slice_bitcast_fusion.1) | copy-start | bytes 8957956
  180.7 1.9 copy-start.7
  180.7 2.2 copy-start.10
  180.7 2.2 copy-start.17
  182.0 100.2 %all-reduce.7.cloned.1.call-start = ((), (), s32[]{:S(2)}) async-start(), calls=%async_computation.2 | async-start | bytes 442368 | tf_op jit(solution)/shard_map/psum | solution.py:166
  196.8 1.6 copy-start.4
  197.0 11.1 %copy-start.8 = (bf16[1,16,8,8,512]{4,3,2,1,0:T(8,128)(2,1)S(1)}, bf16[1,16,8,8,512]{4,3,2,1,0:T(8,128)(2,1)}, u32[]{:S(2)}) copy-start(bf16[1,16,8,8,512]{4,3,2,1,0:T(8,128)(2,1)} %param.4) | copy-start | bytes 3145732
  197.0 11.1 %copy-start.15 = (f32[16]{0:T(128)S(1)}, f32[16]{0:T(128)}, u32[]{:S(2)}) copy-start(f32[16]{0:T(128)} %convert_bitcast_fusion.1) | copy-start | bytes 196
Sparse Core Ops, SparseCore 0:
  182.2 25.7 reduce-scatter.1
  211.4 70.8 all-reduce.6
where the time goes:
time: 296 us; the launch traced here: 291 us
  waiting for transfers between devices  101 us (34%)
  matrix products  62.5 us (21%)
  local copies, waits for them, and re-layouts  51 us (17%)
  other arithmetic  33.8 us (11%)
  starting transfers between devices  20.3 us (7%)
  between operations  14.9 us (5%)
  blocking collectives  7.7 us (3%)
    psum x1, waiting for transfers between devices, local(): grad_part = lax.psum(grad_part, 'space')  70 us
    transpose x1, matrix products, kernel_grad(): return out.transpose(1, 2, 3, 0, 4)  32.2 us
    conv_general_dilated x2, matrix products, conv(): lax.conv_general_dilated(volume[None], kernel, (1, 1, 1), 'VALID', dimens...  30.3 us
    ppermute x6, waiting for transfers between devices, from_behind(): return lax.ppermute(shard, axis, pairs)  23.2 us
    conv_general_dilated x9, local copies, waits for them, and re-layouts, conv(): lax.conv_general_dilated(volume[None], kernel, (1, 1, 1), 'VALID', dimens...  20.1 us
    ppermute x6, starting transfers between devices, from_behind(): return lax.ppermute(shard, axis, pairs)  20 us
    mul x2, local copies, waits for them, and re-layouts, local(): slope_ext = gate_ext * (1.0 + pre_ext * (1.0 - gate_ext))  11.3 us
    all_gather x1, blocking collectives, local(): weight_full = lax.all_gather(weight, 'fsdp', axis=1, tiled=True)  7.7 us
  transfers between devices with their start and end apart: 8, of which 7 were waited for; matrix products, arithmetic and copies ran while one was open for 8% of the time, Pallas kernels for 0%

commit v1 on v0

--- a/solution.py
+++ b/solution.py
@@ -1,3 +1,4 @@
+import functools
 import math
 import jax
 import jax.numpy as jnp
@@ -10,6 +11,35 @@
 PAIR = 2
 DEPTH = 2
 CONV_DIMS = ("NDHWC", "DHWIO", "NDHWC")
+
+
+def draft_tails_over_axis(xs, d0):
+    o_now = list(xs.shape[1:])
+    o_now[d0] *= xs.shape[0]
+    return jnp.moveaxis(xs, 0, d0).reshape(o_now)
+
+
+def _replace_pieces_all(u_in, device_axis, in_dim):
+    n_slots = jax.lax.axis_size(device_axis)
+    slots = list(map(lambda t: (t, (t + 1) % n_slots), range(n_slots)))
+    runs = [(dev, tick) for tick, dev in slots]
+    high, opened = ([], [])
+    for dev_i in tuple(range(n_slots - 1)):
+        if dev_i % 2 == 0:
+            high.append(
+                jax.lax.ppermute(high[-1] if high else u_in, axis_name=device_axis, perm=slots)
+            )
+        else:
+            opened.append(
+                jax.lax.ppermute(opened[-1] if opened else u_in, axis_name=device_axis, perm=runs)
+            )
+    reply = jnp.stack([*high[::-1], u_in, *opened], axis=0)
+    piece_now = jax.lax.axis_index(device_axis) - len(high)
+    reply = reply[(jnp.arange(n_slots) - piece_now) % n_slots]
+    return draft_tails_over_axis(reply, in_dim)
+
+
+map_tiles_on = functools.partial(_replace_pieces_all, device_axis="fsdp", in_dim=1)
 
 
 def from_behind(shard, axis, by):
@@ -132,7 +162,7 @@
         index_now // grid_dims[2] % grid_dims[1],
         index_now % grid_dims[2],
     )
-    weight_full = lax.all_gather(weight, "fsdp", axis=1, tiled=True)
+    weight_full = map_tiles_on(weight)
     k_fwd = super_kernel(weight_full, channels)
     k_back = jnp.flip(k_fwd, (0, 1, 2)).transpose(0, 1, 2, 4, 3)
     present = tissue[0][:, None, None, None] > 0

time: 296 us -> 299 us (1.010)
  blocking collectives: 7.7 us -> 0 us
  starting transfers between devices: 20.3 us -> 25.3 us
  waiting for transfers between devices: 101 us -> 106 us
    all_gather x1 -> x0, blocking collectives: 7.7 us -> none  [local(): weight_full = lax.all_gather(weight, 'fsdp', axis=1, tiled=True)]
    ppermute x6, waiting for transfers between devices: 23.2 us -> 28 us  [from_behind(): return lax.ppermute(shard, axis, pairs)]
    unnamed x40 -> x44, local copies, waits for them, and re-layouts: 6.21 us -> 4.51 us
  transfers between devices with their start and end apart: 8 -> 11, of which waited for: 7 -> 7; matrix products, arithmetic and copies ran while one was open for 8% -> 9% of each run, Pallas kernels for 0% -> 0%
where the time goes in v1:
time: 299 us; the launch traced here: 294 us
  waiting for transfers between devices  106 us (35%)
  matrix products  62.7 us (21%)
  local copies, waits for them, and re-layouts  49.5 us (17%)
  other arithmetic  35.8 us (12%)
  starting transfers between devices  25.3 us (8%)
  between operations  15 us (5%)
    psum x1, waiting for transfers between devices, local(): grad_part = lax.psum(grad_part, 'space')  70 us
    transpose x1, matrix products, kernel_grad(): return out.transpose(1, 2, 3, 0, 4)  32.2 us
    conv_general_dilated x2, matrix products, conv(): lax.conv_general_dilated(volume[None], kernel, (1, 1, 1), 'VALID', dimens...  30.5 us
    ppermute x6, waiting for transfers between devices, from_behind(): return lax.ppermute(shard, axis, pairs)  28 us
    ppermute x6, starting transfers between devices, from_behind(): return lax.ppermute(shard, axis, pairs)  22.4 us
    conv_general_dilated x9, local copies, waits for them, and re-layouts, conv(): lax.conv_general_dilated(volume[None], kernel, (1, 1, 1), 'VALID', dimens...  19.5 us
    mul x2, local copies, waits for them, and re-layouts, local(): slope_ext = gate_ext * (1.0 + pre_ext * (1.0 - gate_ext))  11.3 us
    reduce_scatter x1, waiting for transfers between devices, local(): lax.psum_scatter(grad_term, 'fsdp', scatter_dimension=1, tiled=True)  7.81 us
  transfers between devices with their start and end apart: 11, of which 7 were waited for; matrix products, arithmetic and copies ran while one was open for 9% of the time, Pallas kernels for 0%

profile of v1, /device:TPU:0, one launch (start us, length us, event | category | flops | bytes accessed | tf_op | source)
XLA Modules:
  0.0 294.0 jit_solution(140283622218548682)
XLA Ops:
  7.2 0.0 reduce-scatter.2.cloned.1.call-start
  7.2 0.7 compare_reduce_fusion
  7.9 0.1 gt.24
  8.0 2.7 copy_select_fusion.1
  10.7 1.3 collective-permute-start.1
  12.1 2.5 collective-permute-start.8
  14.5 5.2 %collective-permute-start = (bf16[2,2,16,16,128]{4,3,2,1,0:T(8,128)(2,1)S(1)}, bf16[2,2,16,16,128]{4,3,2,1,0:T(8,128)(2,1)S(1)}, u32[]{:S(2)}, u32[]{:S(2)}) collective-permute-start(bf16[2,2,16,16,128]{4,3,2,1,0:T(8,128)(2,1)S(1)} %get-tuple-element.11), channel_id=1, source_target_pairs={{0,16},{4,20},{8,24},{12,28},{1,17},{5,21},{9,25},{13,29},{2,18},{... | collective-permute-start | bytes 786440 | tf_op jit(solution)/shard_map/ppermute | solution.py:48
  19.7 0.5 convert_bitcast_fusion.1
  20.3 7.7 %collective-permute-done.1 = bf16[2,2,16,16,128]{4,3,2,1,0:T(8,128)(2,1)S(1)} collective-permute-done((bf16[2,2,16,16,128]{4,3,2,1,0:T(8,128)(2,1)S(1)}, bf16[2,2,16,16,128]{4,3,2,1,0:T(8,128)(2,1)S(1)}, u32[]{:S(2)}, u32[]{:S(2)}) %collective-permute-start.1) | collective-permute-done | bytes 262176 | tf_op jit(solution)/shard_map/ppermute | solution.py:48
  28.1 0.9 pad_maximum_fusion.14
  29.0 1.3 collective-permute-start.3
  30.3 0.1 collective-permute-start.7
  30.4 8.8 %collective-permute-start.2 = (bf16[2,20,2,16,128]{4,3,2,1,0:T(8,128)(2,1)}, bf16[2,20,2,16,128]{4,3,2,1,0:T(8,128)(2,1)}, u32[]{:S(2)}, u32[]{:S(2)}) collective-permute-start(bf16[2,20,2,16,128]{4,3,2,1,0:T(8,128)(2,1)} %get-tuple-element.9), channel_id=1, source_target_pairs={{0,8},{4,12},{8,16},{12,20},{16,24},{20,28},{1,9},{5,13},{9,17},{1... | collective-permute-start | bytes 983048 | tf_op jit(solution)/shard_map/ppermute | solution.py:48
  39.2 0.6 copy-done.16
  39.9 1.0 pad_maximum_fusion.2
  40.9 0.6 gather_fusion
  41.6 3.1 %collective-permute-done.3 = bf16[2,20,2,16,128]{4,3,2,1,0:T(8,128)(2,1)} collective-permute-done((bf16[2,20,2,16,128]{4,3,2,1,0:T(8,128)(2,1)}, bf16[2,20,2,16,128]{4,3,2,1,0:T(8,128)(2,1)}, u32[]{:S(2)}, u32[]{:S(2)}) %collective-permute-start.3) | collective-permute-done | bytes 327712 | tf_op jit(solution)/shard_map/ppermute | solution.py:48
  44.6 1.0 broadcast_select_fusion.3
  45.6 1.0 collective-permute-done.2
  46.7 1.9 pad_maximum_fusion.8
  48.6 1.3 collective-permute-start.5
  49.9 0.3 pad_bitcast_fusion.1
  50.3 4.6 %collective-permute-start.4 = (bf16[2,20,20,1,128]{4,3,2,1,0:T(2,128)(2,1)S(1)}, bf16[2,20,20,1,128]{4,3,2,1,0:T(2,128)(2,1)S(1)}, u32[]{:S(2)}, u32[]{:S(2)}) collective-permute-start(bf16[2,20,20,1,128]{4,3,2,1,0:T(2,128)(2,1)S(1)} %get-tuple-element.7), channel_id=1, source_target_pairs={{0,4},{4,8},{8,12},{12,16},{16,20},{20,24},{24,28},{1,5},{5,9},{9,... | collective-permute-start | bytes 614408 | tf_op jit(solution)/shard_map/ppermute | solution.py:48
  54.8 7.3 %collective-permute-done.5 = bf16[2,20,20,1,128]{4,3,2,1,0:T(2,128)(2,1)S(1)} collective-permute-done((bf16[2,20,20,1,128]{4,3,2,1,0:T(2,128)(2,1)S(1)}, bf16[2,20,20,1,128]{4,3,2,1,0:T(2,128)(2,1)S(1)}, u32[]{:S(2)}, u32[]{:S(2)}) %collective-permute-start.5) | collective-permute-done | bytes 204832 | tf_op jit(solution)/shard_map/ppermute | solution.py:48
  62.2 0.4 broadcast_select_fusion.1
  62.6 8.8 %collective-permute-done.4 = bf16[2,20,20,1,128]{4,3,2,1,0:T(2,128)(2,1)S(1)} collective-permute-done((bf16[2,20,20,1,128]{4,3,2,1,0:T(2,128)(2,1)S(1)}, bf16[2,20,20,1,128]{4,3,2,1,0:T(2,128)(2,1)S(1)}, u32[]{:S(2)}, u32[]{:S(2)}) %collective-permute-start.4) | collective-permute-done | bytes 204832 | tf_op jit(solution)/shard_map/ppermute | solution.py:48
  71.5 0.4 broadcast_select_fusion.2
  71.9 5.9 %pad_maximum_fusion = bf16[2,20,20,18,128]{4,3,2,1,0:T(8,128)(2,1)S(1)} fusion(bf16[2,20,20,1,128]{4,3,2,1,0:T(2,128)(2,1)S(1)} %broadcast_select_fusion.1, bf16[2,20,2,16,128]{4,3,2,1,0:T(8,128)(2,1)S(1)} %broadcast_select_fusion.3, bf16[2,2,16,16,128]{4,3,2,1,0:T(8,128)(2,1)S(1)} %broadcast_select_fusion.5, bf16[1,16,16,16,128]{4,3,2,1,0:T(8,128)(2,1)S(1)} %bitcast.96, ...), kind=kLoop, calls=%fused_computation.7 | loop fusion | flops 29491200 | bytes 7372800 | tf_op jit(solution)/shard_map/concatenate | solution.py:93
  77.8 3.0 %fusion.29 = (bf16[20,20,20,128]{3,2,1,0:T(8,128)(2,1)}, bf16[20,20,1,20,128]{4,3,1,0,2:T(8,128)(2,1)S(1)}) fusion(bf16[2,20,20,18,128]{4,3,2,1,0:T(8,128)(2,1)S(1)} %pad_maximum_fusion), kind=kLoop, calls=%fused_computation.40 | loop fusion | bytes 7782400 | tf_op jit(solution)/shard_map/squeeze | solution.py:178
  80.8 0.4 copy.53
  81.2 0.7 pad.9.clone
  81.9 0.3 copy.34
  82.3 0.5 slice.95
  82.8 17.2 %add_multiply_fusion = (f32[18,18,8,3,128]{4,2,3,1,0:T(8,128)}, f32[18,18,8,3,128]{4,2,3,1,0:T(8,128)S(1)}) fusion(bf16[3,3,1,128,128]{4,3,2,1,0:T(8,128)(2,1)S(1)} %get-tuple-element.21, bf16[3,3,1,128,128]{4,3,2,1,0:T(8,128)(2,1)S(1)} %get-tuple-element.20, bf16[3,3,1,128,128]{4,3,2,1,0:T(8,128)(2,1)S(1)} %get-tuple-element.19, ...), kind=kOutput, calls=%fused_computation.18 | convolution fusion | flops 6900842496 | bytes 12738584 | tf_op jit(solution)/shard_map/conv_general_dilated | solution.py:132
  100.0 3.9 %copy.41 = f32[18,18,8,3,128]{4,3,2,1,0:T(4,128)} copy(f32[18,18,8,3,128]{4,2,3,1,0:T(8,128)S(1)} %get-tuple-element.27) | data formatting | bytes 7962624 | tf_op jit(solution)/shard_map/conv_general_dilated | solution.py:132
  103.9 7.3 %reshape.117 = f32[18,18,1,24,128]{4,3,1,0,2:T(8,128)} reshape(f32[18,18,8,3,128]{4,3,2,1,0:T(4,128)} %copy.41) | data formatting | bytes 7962624 | tf_op jit(solution)/shard_map/conv_general_dilated | solution.py:132
  111.3 4.5 %slice_bitcast_fusion.1 = f32[18,18,18,128]{3,2,1,0:T(8,128)} fusion(f32[18,18,1,24,128]{4,3,1,0,2:T(8,128)} %reshape.117), kind=kLoop, calls=%fused_computation.17 | loop fusion | bytes 5971968 | tf_op jit(solution)/shard_map/squeeze | solution.py:132
  115.8 3.0 %add_divide_fusion = f32[18,18,18,128]{3,2,1,0:T(8,128)} fusion(f32[18,18,1,24,128]{4,3,1,0,2:T(8,128)S(1)} %copy-done.1), kind=kLoop, calls=%fused_computation.19 | loop fusion | flops 2239488 | bytes 5971968 | tf_op jit(solution)/shard_map/div | solution.py:181
  118.8 3.9 %convert_bitcast_fusion = f32[18,18,18,128]{3,2,1,0:T(8,128)} fusion(bf16[2,20,20,18,128]{4,3,2,1,0:T(8,128)(2,1)} %copy-done), kind=kLoop, calls=%fused_computation.5 | loop fusion | flops 746496 | bytes 4478976 | tf_op jit(solution)/shard_map/convert_element_type | solution.py:183
  122.7 3.9 %copy.43 = f32[18,18,8,3,128]{4,3,2,1,0:T(4,128)} copy(f32[18,18,8,3,128]{4,2,3,1,0:T(8,128)S(1)} %copy-done.10) | data formatting | bytes 7962624 | tf_op jit(solution)/shard_map/mul | solution.py:182
  126.6 7.3 %reshape.126 = f32[18,18,1,24,128]{4,3,1,0,2:T(8,128)} reshape(f32[18,18,8,3,128]{4,3,2,1,0:T(4,128)} %copy.43) | data formatting | bytes 7962624 | tf_op jit(solution)/shard_map/mul | solution.py:182
  133.9 3.2 %fusion.22 = bf16[18,18,1,18,128]{4,3,1,0,2:T(8,128)(2,1)S(1)} fusion(f32[18,18,1,24,128]{4,3,1,0,2:T(8,128)} %reshape.126, bf16[2,20,20,18,128]{4,3,2,1,0:T(8,128)(2,1)} %copy-done), kind=kLoop, calls=%fused_computation.34 | loop fusion | flops 2239488 | bytes 5971968 | tf_op jit(solution)/shard_map/convert_element_type | solution.py:183
  137.1 0.4 pad.11
  137.4 3.0 %reshape.120 = bf16[18,18,1,8,3,128]{5,4,3,1,0,2:T(4,128)(2,1)} reshape(bf16[18,18,1,24,128]{4,3,1,0,2:T(8,128)(2,1)S(1)} %pad.11) | data formatting | bytes 3981312 | tf_op jit(solution)/shard_map/conv_general_dilated | solution.py:132
  140.4 2.2 copy.45
  142.7 1.5 slice.104
  144.2 1.1 slice_bitcast_fusion.2
  145.3 1.2 copy-done.2
  146.5 4.3 %fusion.31 = (bf16[1,16,16,16,128]{4,3,2,1,0:T(8,128)(2,1)S(1)}, f32[16,16,16,128]{3,2,1,0:T(8,128)}) fusion(f32[18,18,18,128]{3,2,1,0:T(8,128)S(1)} %copy-done.2, f32[18,18,18,128]{3,2,1,0:T(8,128)S(1)} %copy-done.3, f32[18,18,18,128]{3,2,1,0:T(8,128)} %convert_bitcast_fusion), kind=kLoop, calls=%fused_computation.42 | loop fusion | flops 3670016 | bytes 9437184 | tf_op jit(solution)/shard_map/broadcast_in_dim | solution.py:145
  150.8 32.2 %fusion.17 = f32[3,3,3,128,128]{4,3,2,1,0:T(8,128)S(1)} fusion(bf16[1,18,18,18,128]{4,3,2,1,0:T(8,128)(2,1)S(1)} %slice_bitcast_fusion.2, bf16[1,16,16,16,128]{4,3,2,1,0:T(8,128)(2,1)S(1)} %get-tuple-element.3), kind=kOutput, calls=%fused_computation.26 | convolution fusion | flops 3623878656 | bytes 4311040 | tf_op jit(solution)/shard_map/transpose | solution.py:151
  183.1 0.3 slice_add_fusion.2
  183.4 1.0 maximum_multiply_fusion
  184.4 0.3 all-reduce.7.cloned.1.call-start
  184.7 0.2 copy-done.8
  184.9 0.4 copy-done.11
  185.3 13.3 %fusion.25 = f32[16,16,8,3,128]{4,2,3,1,0:T(8,128)S(1)} fusion(bf16[18,18,1,7,2,128]{5,3,4,1,0,2:T(8,128)(2,1)S(1)} %copy-done.11, bf16[18,18,1,8,3,128]{5,3,4,1,0,2:T(8,128)(2,1)S(1)} %copy-done.8, pred[8,3]{0,1:T(4,128)(4,1)S(1)} %copy-done.19, bf16[3,3,1,128,128]{4,3,2,1,0:T(8,128)(2,1)} %copy-done.14, bf16[3,3,1,128,128]{4,3,2,1,0:T(8,128)(2,1)} %copy-done.13, ...), kind=kOutput, calls=%fused_computation.38 | convolution fusion | flops 5447442432 | bytes 7182360 | tf_op jit(solution)/shard_map/conv_general_dilated | solution.py:132
  198.6 0.5 copy.46
  199.2 0.2 slice.105
  199.4 1.6 copy.47
  201.0 2.0 copy.42
  203.0 7.8 %reduce-scatter.2.cloned.1.call-done = f32[27,16,64]{2,1,0:T(8,128)} async-done(((f32[27,64,64]{2,1,0:T(8,128)}), f32[27,16,64]{2,1,0:T(8,128)}) %reduce-scatter.2.cloned.1.call-update) | async-done | bytes 110608 | tf_op jit(solution)/shard_map/reduce_scatter | solution.py:195
  210.9 4.2 %multiply_convert_fusion = (bf16[1,16,8,8,512]{4,3,2,1,0:T(8,128)(2,1)}, bf16[1,16,8,8,512]{4,3,2,1,0:T(8,128)(2,1)}) fusion(f32[1,16,8,8,512]{4,3,2,1,0:T(8,128)S(1)} %bitcast.101, bf16[1,16,8,8,512]{4,3,2,1,0:T(8,128)(2,1)} %param.5, f32[16]{0:T(128)S(1)} %copy-done.17, f32[1,16,8,8,512]{4,3,2,1,0:T(8,128)} %bitcast.102, ...), kind=kLoop, calls=%fused_computation.30 | loop fusion | flops 4194304 | bytes 8388672 | tf_op jit(solution)/shard_map/convert_element_type | solution.py:189
  215.2 70.0 %all-reduce.7.cloned.1.call-done = f32[27,16,64]{2,1,0:T(8,128)} async-done(((f32[27,16,64]{2,1,0:T(8,128)}), f32[27,16,64]{2,1,0:T(8,128)}) %all-reduce.7.cloned.1.call-update) | async-done | bytes 110608 | tf_op jit(solution)/shard_map/psum | solution.py:196
  285.1 1.6 copy.61
  (53 shorter events, 0.3 us)
Async XLA Ops:
  7.2 12.6 %copy-start.18 = (s32[1,16]{1,0:T(1,128)S(1)}, s32[1,16]{1,0:T(1,128)}, u32[]{:S(2)}) copy-start(s32[1,16]{1,0:T(1,128)} %param.6) | copy-start | bytes 196
  7.2 4.9 %copy-start.15 = (bf16[27,16,64]{2,1,0:T(8,128)(2,1)S(1)}, bf16[27,16,64]{2,1,0:T(8,128)(2,1)}, u32[]{:S(2)}) copy-start(bf16[27,16,64]{2,1,0:T(8,128)(2,1)} %param.7) | copy-start | bytes 165892
  7.2 203.7 %reduce-scatter.2.cloned.1.call-start = ((), (), s32[]{:S(2)}) async-start(), calls=%async_computation.1 | async-start | bytes 1105920 | tf_op jit(solution)/shard_map/reduce_scatter | solution.py:195
  10.7 17.3 %collective-permute-start.1 = (bf16[2,2,16,16,128]{4,3,2,1,0:T(8,128)(2,1)S(1)}, bf16[2,2,16,16,128]{4,3,2,1,0:T(8,128)(2,1)S(1)}, u32[]{:S(2)}, u32[]{:S(2)}) collective-permute-start(bf16[2,2,16,16,128]{4,3,2,1,0:T(8,128)(2,1)S(1)} %get-tuple-element.12), channel_id=1, source_target_pairs={{16,0},{20,4},{24,8},{28,12},{17,1},{21,5},{25,9},{29,13},{18,2},{... | collective-permute-start | bytes 786440 | tf_op jit(solution)/shard_map/ppermute | solution.py:48
  12.1 27.2 %collective-permute-start.8 = (bf16[27,16,64]{2,1,0:T(8,128)(2,1)S(1)}, bf16[27,16,64]{2,1,0:T(8,128)(2,1)S(1)}, u32[]{:S(2)}, u32[]{:S(2)}) collective-permute-start(bf16[27,16,64]{2,1,0:T(8,128)(2,1)S(1)} %copy-done.15), channel_id=1, source_target_pairs={{1,0},{2,1},{3,2},{0,3},{5,4},{6,5},{7,6},{4,7},{9,8},{10,9},{11,1... | collective-permute-start | bytes 165896 | tf_op jit(solution)/shard_map/ppermute | solution.py:34
  14.5 15.8 %collective-permute-start.6 = (bf16[27,16,64]{2,1,0:T(8,128)(2,1)S(1)}, bf16[27,16,64]{2,1,0:T(8,128)(2,1)S(1)}, u32[]{:S(2)}, u32[]{:S(2)}) collective-permute-start(bf16[27,16,64]{2,1,0:T(8,128)(2,1)S(1)} %copy-done.15), channel_id=1, source_target_pairs={{0,1},{1,2},{2,3},{3,0},{4,5},{5,6},{6,7},{7,4},{8,9},{9,10},{10,1... | collective-permute-start | bytes 165896 | tf_op jit(solution)/shard_map/ppermute | solution.py:30
  14.5 13.5 %collective-permute-start = (bf16[2,2,16,16,128]{4,3,2,1,0:T(8,128)(2,1)S(1)}, bf16[2,2,16,16,128]{4,3,2,1,0:T(8,128)(2,1)S(1)}, u32[]{:S(2)}, u32[]{:S(2)}) collective-permute-start(bf16[2,2,16,16,128]{4,3,2,1,0:T(8,128)(2,1)S(1)} %get-tuple-element.11), channel_id=1, source_target_pairs={{0,16},{4,20},{8,24},{12,28},{1,17},{5,21},{9,25},{13,29},{2,18},{... | collective-permute-start | bytes 786440 | tf_op jit(solution)/shard_map/ppermute | solution.py:48
  29.0 15.6 %collective-permute-start.3 = (bf16[2,20,2,16,128]{4,3,2,1,0:T(8,128)(2,1)}, bf16[2,20,2,16,128]{4,3,2,1,0:T(8,128)(2,1)}, u32[]{:S(2)}, u32[]{:S(2)}) collective-permute-start(bf16[2,20,2,16,128]{4,3,2,1,0:T(8,128)(2,1)} %get-tuple-element.10), channel_id=1, source_target_pairs={{8,0},{12,4},{16,8},{20,12},{24,16},{28,20},{9,1},{13,5},{17,9},{2... | collective-permute-start | bytes 983048 | tf_op jit(solution)/shard_map/ppermute | solution.py:48
  30.3 8.9 %collective-permute-start.7 = (bf16[27,16,64]{2,1,0:T(8,128)(2,1)S(1)}, bf16[27,16,64]{2,1,0:T(8,128)(2,1)S(1)}, u32[]{:S(2)}, u32[]{:S(2)}) collective-permute-start(bf16[27,16,64]{2,1,0:T(8,128)(2,1)S(1)} %collective-permute-done.6), channel_id=1, source_target_pairs={{0,1},{1,2},{2,3},{3,0},{4,5},{5,6},{6,7},{7,4},{8,9},{9,10},{10,1... | collective-permute-start | bytes 165896 | tf_op jit(solution)/shard_map/ppermute | solution.py:30
  30.4 16.2 %collective-permute-start.2 = (bf16[2,20,2,16,128]{4,3,2,1,0:T(8,128)(2,1)}, bf16[2,20,2,16,128]{4,3,2,1,0:T(8,128)(2,1)}, u32[]{:S(2)}, u32[]{:S(2)}) collective-permute-start(bf16[2,20,2,16,128]{4,3,2,1,0:T(8,128)(2,1)} %get-tuple-element.9), channel_id=1, source_target_pairs={{0,8},{4,12},{8,16},{12,20},{16,24},{20,28},{1,9},{5,13},{9,17},{1... | collective-permute-start | bytes 983048 | tf_op jit(solution)/shard_map/ppermute | solution.py:48
  39.2 0.6 copy-start.16
  48.6 13.6 %collective-permute-start.5 = (bf16[2,20,20,1,128]{4,3,2,1,0:T(2,128)(2,1)S(1)}, bf16[2,20,20,1,128]{4,3,2,1,0:T(2,128)(2,1)S(1)}, u32[]{:S(2)}, u32[]{:S(2)}) collective-permute-start(bf16[2,20,20,1,128]{4,3,2,1,0:T(2,128)(2,1)S(1)} %get-tuple-element.8), channel_id=1, source_target_pairs={{4,0},{8,4},{12,8},{16,12},{20,16},{24,20},{28,24},{5,1},{9,5},{13... | collective-permute-start | bytes 614408 | tf_op jit(solution)/shard_map/ppermute | solution.py:48
  50.2 32.5 %copy-start.12 = (bf16[3,3,1,128,128]{4,3,2,1,0:T(8,128)(2,1)}, bf16[3,3,1,128,128]{4,3,2,1,0:T(8,128)(2,1)S(1)}, u32[]{:S(2)}) copy-start(bf16[3,3,1,128,128]{4,3,2,1,0:T(8,128)(2,1)S(1)} %get-tuple-element.19) | copy-start | bytes 884740
  50.2 32.5 %copy-start.13 = (bf16[3,3,1,128,128]{4,3,2,1,0:T(8,128)(2,1)}, bf16[3,3,1,128,128]{4,3,2,1,0:T(8,128)(2,1)S(1)}, u32[]{:S(2)}) copy-start(bf16[3,3,1,128,128]{4,3,2,1,0:T(8,128)(2,1)S(1)} %get-tuple-element.20) | copy-start | bytes 884740
  50.3 32.5 %copy-start.14 = (bf16[3,3,1,128,128]{4,3,2,1,0:T(8,128)(2,1)}, bf16[3,3,1,128,128]{4,3,2,1,0:T(8,128)(2,1)S(1)}, u32[]{:S(2)}) copy-start(bf16[3,3,1,128,128]{4,3,2,1,0:T(8,128)(2,1)S(1)} %get-tuple-element.21) | copy-start | bytes 884740
  50.3 21.2 %collective-permute-start.4 = (bf16[2,20,20,1,128]{4,3,2,1,0:T(2,128)(2,1)S(1)}, bf16[2,20,20,1,128]{4,3,2,1,0:T(2,128)(2,1)S(1)}, u32[]{:S(2)}, u32[]{:S(2)}) collective-permute-start(bf16[2,20,20,1,128]{4,3,2,1,0:T(2,128)(2,1)S(1)} %get-tuple-element.7), channel_id=1, source_target_pairs={{0,4},{4,8},{8,12},{12,16},{16,20},{20,24},{24,28},{1,5},{5,9},{9,... | collective-permute-start | bytes 614408 | tf_op jit(solution)/shard_map/ppermute | solution.py:48
  77.8 3.0 %copy-start = (bf16[2,20,20,18,128]{4,3,2,1,0:T(8,128)(2,1)}, bf16[2,20,20,18,128]{4,3,2,1,0:T(8,128)(2,1)S(1)}, u32[]{:S(2)}) copy-start(bf16[2,20,20,18,128]{4,3,2,1,0:T(8,128)(2,1)S(1)} %pad_maximum_fusion) | copy-start | bytes 11059204
  81.9 0.8 copy-start.20
  111.3 4.5 %copy-start.1 = (f32[18,18,1,24,128]{4,3,1,0,2:T(8,128)S(1)}, f32[18,18,1,24,128]{4,3,1,0,2:T(8,128)}, u32[]{:S(2)}) copy-start(f32[18,18,1,24,128]{4,3,1,0,2:T(8,128)} %reshape.117) | copy-start | bytes 11943940
  118.8 3.9 %copy-start.10 = (f32[18,18,8,3,128]{4,2,3,1,0:T(8,128)S(1)}, f32[18,18,8,3,128]{4,2,3,1,0:T(8,128)}, u32[]{:S(2)}) copy-start(f32[18,18,8,3,128]{4,2,3,1,0:T(8,128)} %get-tuple-element.26) | copy-start | bytes 11943940
  140.4 3.7 %copy-start.6 = (bf16[20,20,20,128]{3,2,1,0:T(8,128)(2,1)S(1)}, bf16[20,20,20,128]{3,2,1,0:T(8,128)(2,1)}, u32[]{:S(2)}) copy-start(bf16[20,20,20,128]{3,2,1,0:T(8,128)(2,1)} %get-tuple-element.5) | copy-start | bytes 6144004
  140.4 4.9 %copy-start.3 = (f32[18,18,18,128]{3,2,1,0:T(8,128)S(1)}, f32[18,18,18,128]{3,2,1,0:T(8,128)}, u32[]{:S(2)}) copy-start(f32[18,18,18,128]{3,2,1,0:T(8,128)} %add_divide_fusion) | copy-start | bytes 8957956
  142.7 8.1 %copy-start.7 = (bf16[18,18,1,8,3,128]{5,3,4,1,0,2:T(8,128)(2,1)}, bf16[18,18,1,8,3,128]{5,3,4,1,0,2:T(8,128)(2,1)S(1)}, u32[]{:S(2)}) copy-start(bf16[18,18,1,8,3,128]{5,3,4,1,0,2:T(8,128)(2,1)S(1)} %copy.45) | copy-start | bytes 5971972
  142.7 3.8 %copy-start.2 = (f32[18,18,18,128]{3,2,1,0:T(8,128)S(1)}, f32[18,18,18,128]{3,2,1,0:T(8,128)}, u32[]{:S(2)}) copy-start(f32[18,18,18,128]{3,2,1,0:T(8,128)} %slice_bitcast_fusion.1) | copy-start | bytes 8957956
  183.0 1.9 copy-start.8
  183.1 2.2 copy-start.11
  183.1 2.2 copy-start.19
  184.4 100.7 %all-reduce.7.cloned.1.call-start = ((), (), s32[]{:S(2)}) async-start(), calls=%async_computation.2 | async-start | bytes 442368 | tf_op jit(solution)/shard_map/psum | solution.py:196
  199.2 1.9 copy-start.4
  199.4 11.5 %copy-start.9 = (bf16[1,16,8,8,512]{4,3,2,1,0:T(8,128)(2,1)S(1)}, bf16[1,16,8,8,512]{4,3,2,1,0:T(8,128)(2,1)}, u32[]{:S(2)}) copy-start(bf16[1,16,8,8,512]{4,3,2,1,0:T(8,128)(2,1)} %param.4) | copy-start | bytes 3145732
  199.4 11.5 %copy-start.17 = (f32[16]{0:T(128)S(1)}, f32[16]{0:T(128)}, u32[]{:S(2)}) copy-start(f32[16]{0:T(128)} %convert_bitcast_fusion.1) | copy-start | bytes 196
  201.0 9.9 %copy-start.5 = (f32[2,2,4,8,8,4,128]{6,4,5,3,2,1,0:T(8,128)S(1)}, f32[2,2,4,8,8,4,128]{6,4,5,3,2,1,0:T(8,128)}, u32[]{:S(2)}) copy-start(f32[2,2,4,8,8,4,128]{6,4,5,3,2,1,0:T(8,128)} %copy.47) | copy-start | bytes 6291460
Sparse Core Ops, SparseCore 0:
  184.5 26.2 reduce-scatter.1
  214.2 70.8 all-reduce.6
